TPU v7x, 512 devices: a whole 4x8x8 slice. The times are simulated.
512 devices in a mesh: slab: 64 (over z, x, core), obs: 8 (over y).
Axes of the slice: x: 4, y: 8, z: 8, core: 2. Of those that a mesh axis runs over, the one named last changes fastest.
Arguments:
- background_members: float32 [64, 1048576], P('slab', 'obs'), may hold values from -6 to 6
- measurement_jitter: bfloat16 [64, 8, 65536], P(None, 'obs', 'slab'), may hold values from -5 to 5
- measurement_readings: float32 [8, 65536], P('obs', 'slab'), may hold values from -8 to 8
- measurement_noise_spread: float32 [8, 65536], P('obs', 'slab'), may hold values from 0.2 to 2
- measurement_grid_location: int32 [8, 65536], P('obs', 'slab'), may hold values from 0 to 2047
- active_tallies: int32 [8, 64], P('obs', 'slab'), may hold values from 128 to 1024, as said below
- coupling_listing: int32 [8, 2048, 8], P('obs', 'slab'), may hold values from 0 to 63, as said below
- taper_factors: float32 [8, 2048, 8], P('obs', 'slab'), may hold values from 0.1 to 1
Outputs:
- analysis: float32 [64, 1048576], P('slab', 'obs')
Inputs may be any that keep to these rules, and one draw needn't show every extreme that they name: `active_tallies`: some region of some group holds 1024 live observations; slots beyond a region's count are padding. `coupling_listing`: the 8 observation blocks listed for a state block are distinct.
All inputs are finite; a program needn't handle non-finite values.
Results may differ from a plain program's by a relative error of at most 0.0063.
Values may be sent and summed in bfloat16 or wider, within the bound.
No kernel may reach another device: no remote copies, remote signals or barrier semaphores. Data moves between devices by JAX's collectives and lax.ppermute only.
A program may use at most 64 MiB of HBM per device.

v0:
```python
import jax
import jax.numpy as jnp
from jax import lax
from jax.sharding import PartitionSpec as P

OB = 128
highest = lax.Precision.HIGHEST


def block_products(
    tile_work,
    measurement_jitter,
    measurement_readings,
    measurement_noise_spread,
    measurement_grid_location,
    active_tallies,
):
    members = tile_work.shape[0]
    positions = measurement_grid_location[0]
    obs_count = positions.shape[0]
    prior_value = jnp.take(tile_work, positions, axis=1)
    prior_shift = prior_value - jnp.mean(prior_value, axis=0, keepdims=True)
    spread = jnp.sum(prior_shift * prior_shift, axis=0, keepdims=True) / (members - 1)
    usable = jnp.arange(obs_count, dtype=jnp.int32)[None, :] < active_tallies[0, 0]
    innovation = (
        measurement_readings + measurement_jitter[:, 0, :].astype(jnp.float32) - prior_value
    ) / (spread + measurement_noise_spread)
    gain_input = jnp.where(usable, innovation, jnp.float32(0.0)).astype(jnp.bfloat16)
    prior_low = prior_shift.astype(jnp.bfloat16)
    return jnp.einsum(
        "mco,nco->cmn",
        gain_input.reshape(members, -1, OB),
        prior_low.reshape(members, -1, OB),
        preferred_element_type=jnp.float32,
    )


def local(
    background_members,
    measurement_jitter,
    measurement_readings,
    measurement_noise_spread,
    measurement_grid_location,
    active_tallies,
    coupling_listing,
    taper_factors,
):
    work_low = background_members.astype(jnp.bfloat16)
    tile_low = lax.all_to_all(work_low, "slab", split_axis=1, concat_axis=0, tiled=True)
    tile_work = tile_low.astype(jnp.float32)
    members = tile_work.shape[0]
    blocks = coupling_listing.shape[1]
    deviation = tile_work - jnp.mean(tile_work, axis=0, keepdims=True)
    products = block_products(
        tile_work,
        measurement_jitter,
        measurement_readings,
        measurement_noise_spread,
        measurement_grid_location,
        active_tallies,
    )
    all_products = lax.all_gather(products, "obs", axis=0, tiled=True)
    obs_blocks = all_products.shape[0]
    block_links = coupling_listing[0]
    factor = taper_factors[0] / (members - 1)
    choose = block_links[..., None] == jnp.arange(obs_blocks, dtype=jnp.int32)
    localize = jnp.sum(jnp.where(choose, factor[..., None], jnp.float32(0.0)), axis=1)
    ensemble = jnp.einsum("bc,cmn->bmn", localize, all_products, precision=highest)
    region_dev = deviation.reshape(members, blocks, -1)
    increment = jnp.einsum("bmn,nbp->mbp", ensemble, region_dev, precision=highest)
    increment_low = increment.reshape(members, -1).astype(jnp.bfloat16)
    back = lax.all_to_all(increment_low, "slab", split_axis=0, concat_axis=1, tiled=True)
    return background_members + back.astype(jnp.float32)


def solution(mesh):
    return jax.shard_map(
        local,
        mesh=mesh,
        in_specs=(
            P("slab", "obs"),
            P(None, "obs", "slab"),
            P("obs", "slab"),
            P("obs", "slab"),
            P("obs", "slab"),
            P("obs", "slab"),
            P("obs", "slab", None),
            P("obs", "slab", None),
        ),
        out_specs=P("slab", "obs"),
        check_vma=False,
    )
```

profile of v0, /device:TPU:1, one launch (start us, length us, event | category | flops | bytes accessed | tf_op | source)
XLA Modules:
  0.0 124.3 jit_solution(9766494422847316278)
XLA Ops:
  6.5 0.0 copy-start.1
  6.5 0.0 copy-start.2
  6.5 1.4 %convert_element_type.60 = bf16[1,131072]{1,0:T(2,128)(2,1)S(1)} convert(f32[1,131072]{1,0:T(1,128)} %param.8) | non-fusion elementwise | flops 131072 | bytes 786432 | tf_op jit(solution)/shard_map/convert_element_type | solution.py:48
  8.0 0.5 broadcast.91
  8.5 2.1 %reduce.1 = bf16[64,2048]{1,0:T(8,128)(2,1)S(1)} reduce(bf16[64,1,2048]{2,1,0:T(2,128)(2,1)S(1)} %bitcast.46, bf16[]{:T(256)} %broadcast.91), dimensions={1}, to_apply=%bitcast.40.reduce_sub_computation | reduce | bytes 524290
  10.6 0.9 reshape.167
  11.5 14.8 %all-to-all-start = ((bf16[64,2,1024]{2,1,0:T(2,128)(2,1)}), bf16[64,2,1024]{2,1,0:T(2,128)(2,1)S(1)}, u32[]{:S(2)}, u32[]{:S(2)}) async-start(bf16[64,2,1024]{2,1,0:T(2,128)(2,1)} %reshape.167), calls=%async_computation | async-start | bytes 524288 | tf_op jit(solution)/shard_map/all_to_all | solution.py:49
  26.3 0.0 all-gather.2.cloned.1.call-start
  27.0 0.0 copy-done.1
  27.1 0.0 copy-done.2
  27.2 12.2 %all-to-all-done = bf16[64,2,1024]{2,1,0:T(2,128)(2,1)S(1)} async-done(((bf16[64,2,1024]{2,1,0:T(2,128)(2,1)}), bf16[64,2,1024]{2,1,0:T(2,128)(2,1)S(1)}, u32[]{:S(2)}, u32[]{:S(2)}) %all-to-all-start) | async-done | bytes 262176 | tf_op jit(solution)/shard_map/all_to_all | solution.py:49
  39.4 0.2 reshape.168
  39.7 0.5 copy.28
  40.2 0.1 convert_bitcast_fusion
  40.3 0.0 copy-start.3
  40.3 0.0 copy-start.6
  40.3 2.8 %gather_fusion = f32[1024,64]{1,0:T(8,128)S(1)} fusion(f32[64,2048]{0,1:T(8,128)S(1)} %convert_bitcast_fusion, s32[1024]{0:T(1024)S(1)} %broadcast_clamp_fusion), kind=kCustom, calls=%fused_computation | custom fusion | bytes 528384 | tf_op jit(solution)/shard_map/jit(_take)/gather | solution.py:21
  43.1 0.0 copy-start.5
  43.1 0.0 copy-start.4
  43.1 0.4 fusion.5
  43.5 0.5 multiply_reduce_fusion
  44.0 0.2 copy.32
  44.2 0.0 copy-done.3
  44.2 0.0 copy-done.6
  44.2 0.9 fusion.10
  45.2 0.0 all-gather.2.cloned.1.call-update
  45.2 0.0 copy-done.5
  45.2 0.1 copy.30
  45.3 0.0 copy-done.4
  45.3 0.1 copy.29
  45.4 0.1 select_reduce_fusion
  45.5 0.2 convert_reduce_fusion
  45.7 0.1 div.45
  45.8 34.1 %all-gather.2.cloned.1.call-done = f32[64,64,64]{2,1,0:T(8,128)} async-done(((f32[8,64,64]{2,1,0:T(8,128)}), f32[64,64,64]{2,1,0:T(8,128)}) %all-gather.2.cloned.1.call-update) | async-done | bytes 1048592 | tf_op jit(solution)/shard_map/all_gather | solution.py:62
  80.0 3.9 %fusion = f32[32,64,64]{2,0,1:T(8,128)S(1)} fusion(f32[64,64,64]{2,1,0:T(8,128)} %all-gather.2.cloned.1.call-done, f32[32,64]{1,0:T(8,128)S(1)} %select_reduce_fusion), kind=kOutput, calls=%fused_computation.1 | convolution fusion | flops 100663296 | bytes 1581056 | tf_op jit(solution)/shard_map/bc,cmn->bmn/dot_general | solution.py:68
  83.8 2.3 %convolution_convert_fusion = bf16[32,64,64]{2,1,0:T(8,128)(2,1)S(1)} fusion(f32[32,64,64]{2,0,1:T(8,128)S(1)} %fusion, f32[32,64]{1,0:T(8,128)S(1)} %div.45, bf16[64,32,64]{0,2,1:T(8,128)(2,1)S(1)} %bitcast.43), kind=kOutput, calls=%fused_computation.3 | convolution fusion | flops 101056512 | bytes 1056768 | tf_op jit(solution)/shard_map/bmn,nbp->mbp/dot_general | solution.py:70
  86.2 0.0 copy-start
  86.2 1.1 reduce.2
  87.3 0.2 copy.51
  87.5 0.2 reshape.169
  87.7 28.1 %all_to_all.23 = bf16[64,2,1024]{2,1,0:T(2,128)(2,1)S(1)} all-to-all(bf16[64,2,1024]{2,1,0:T(2,128)(2,1)S(1)} %reshape.169), channel_id=1, replica_groups=mesh['slab'=64,'obs'=8] {'slab'}, dimensions={0} | all-to-all | bytes 524288 | tf_op jit(solution)/shard_map/all_to_all | solution.py:72
  115.8 0.2 reshape.170
  116.0 0.0 copy-done
  116.0 1.5 %convert_add_fusion = f32[1,131072]{1,0:T(1,128)} fusion(f32[1,131072]{1,0:T(1,128)S(1)} %copy-done, bf16[1,131072]{1,0:T(2,128)(2,1)S(1)} %bitcast.45), kind=kLoop, calls=%fused_computation.6 | loop fusion | flops 262144 | bytes 1310720 | tf_op jit(solution)/shard_map/add | solution.py:73
  (11 shorter events, 0.1 us)
Async XLA Ops:
  6.5 20.5 %copy-start.1 = (bf16[64,1,1024]{2,0,1:T(8,128)(2,1)S(1)}, bf16[64,1,1024]{2,0,1:T(8,128)(2,1)}, u32[]{:S(2)}) copy-start(bf16[64,1,1024]{2,0,1:T(8,128)(2,1)} %param.9) | copy-start | bytes 393220
  6.5 20.5 %copy-start.2 = (s32[1,1024]{1,0:T(1,128)S(1)}, s32[1,1024]{1,0:T(1,128)}, u32[]{:S(2)}) copy-start(s32[1,1024]{1,0:T(1,128)} %param.12) | copy-start | bytes 12292
  11.5 27.9 %all-to-all-start = ((bf16[64,2,1024]{2,1,0:T(2,128)(2,1)}), bf16[64,2,1024]{2,1,0:T(2,128)(2,1)S(1)}, u32[]{:S(2)}, u32[]{:S(2)}) async-start(bf16[64,2,1024]{2,1,0:T(2,128)(2,1)} %reshape.167), calls=%async_computation | async-start | bytes 524288 | tf_op jit(solution)/shard_map/all_to_all | solution.py:49
  26.3 53.6 %all-gather.2.cloned.1.call-start = ((), (), s32[]{:S(2)}) async-start(), calls=%async_computation.2 | async-start | bytes 2359296 | tf_op jit(solution)/shard_map/all_gather | solution.py:62
  40.3 4.0 %copy-start.3 = (f32[1,1024]{1,0:T(1,128)S(1)}, f32[1,1024]{1,0:T(1,128)}, u32[]{:S(2)}) copy-start(f32[1,1024]{1,0:T(1,128)} %param.11) | copy-start | bytes 12292
  40.3 4.0 %copy-start.6 = (f32[1,1024]{1,0:T(1,128)S(1)}, f32[1,1024]{1,0:T(1,128)}, u32[]{:S(2)}) copy-start(f32[1,1024]{1,0:T(1,128)} %param.10) | copy-start | bytes 12292
  43.1 2.1 %copy-start.5 = (f32[1,32,8]{1,2,0:T(8,128)S(1)}, f32[1,32,8]{1,2,0:T(8,128)}, u32[]{:S(2)}) copy-start(f32[1,32,8]{1,2,0:T(8,128)} %param.15) | copy-start | bytes 3076
  43.1 2.2 %copy-start.4 = (s32[1,32,8]{1,2,0:T(8,128)S(1)}, s32[1,32,8]{1,2,0:T(8,128)}, u32[]{:S(2)}) copy-start(s32[1,32,8]{1,2,0:T(8,128)} %param.14) | copy-start | bytes 3076
  86.2 29.8 %copy-start = (f32[1,131072]{1,0:T(1,128)S(1)}, f32[1,131072]{1,0:T(1,128)}, u32[]{:S(2)}) copy-start(f32[1,131072]{1,0:T(1,128)} %param.8) | copy-start | bytes 1572868
Sparse Core Ops, SparseCore 0:
  45.3 34.6 all-gather.1
where the time goes:
time: 125 us; the launch traced here: 124 us
  waiting for transfers between devices  46.4 us (37%)
  blocking collectives  28.1 us (22%)
  starting transfers between devices  14.9 us (12%)
  between operations  14.3 us (11%)
  other arithmetic  7.54 us (6%)
  matrix products  7.11 us (6%)
  local copies, waits for them, and re-layouts  6.04 us (5%)
    all_gather x1, waiting for transfers between devices, local(): all_products = lax.all_gather(products, 'obs', axis=0, tiled=True)  34.1 us
    all_to_all x1, blocking collectives, local(): lax.all_to_all(increment_low, 'slab', split_axis=0, concat_axis=1, tiled=...  28.1 us
    all_to_all x1, starting transfers between devices, local(): lax.all_to_all(work_low, 'slab', split_axis=1, concat_axis=0, tiled=True)  14.8 us
    all_to_all x1, waiting for transfers between devices, local(): lax.all_to_all(work_low, 'slab', split_axis=1, concat_axis=0, tiled=True)  12.2 us
    dot_general x1, matrix products, local(): jnp.einsum('bc,cmn->bmn', localize, all_products, precision=highest)  3.85 us
    gather x2, local copies, waits for them, and re-layouts, block_products(): prior_value = jnp.take(tile_work, positions, axis=1)  2.99 us
  transfers between devices with their start and end apart: 2, of which 2 were waited for; matrix products, arithmetic and copies ran while one was open for 1% of the time, Pallas kernels for 0%

commit v1 on v0

--- a/solution.py
+++ b/solution.py
@@ -5,6 +5,28 @@
 
 OB = 128
 highest = lax.Precision.HIGHEST
+
+
+def in_order(blocks, dim):
+    blocks = jnp.moveaxis(blocks, 0, dim)
+    shape = blocks.shape
+    return blocks.reshape(*shape[:dim], shape[dim] * shape[dim + 1], *shape[dim + 2 :])
+
+
+def gather_around(x, axis, dim):
+    devices = lax.axis_size(axis)
+    pairs = [(i, (i + 1) % devices) for i in range(devices)]
+    back = [(b, a) for a, b in pairs]
+    lower, upper = ([], [])
+    for step in range(devices - 1):
+        if step % 2 == 0:
+            lower.append(lax.ppermute(lower[-1] if lower else x, axis, pairs))
+        else:
+            upper.append(lax.ppermute(upper[-1] if upper else x, axis, back))
+    tiles = jnp.stack([*lower[::-1], x, *upper])
+    shift = lax.axis_index(axis) - len(lower)
+    tiles = tiles[(jnp.arange(devices) - shift) % devices]
+    return in_order(tiles, dim)
 
 
 def block_products(
@@ -59,7 +81,7 @@
         measurement_grid_location,
         active_tallies,
     )
-    all_products = lax.all_gather(products, "obs", axis=0, tiled=True)
+    all_products = gather_around(products, "obs", 0)
     obs_blocks = all_products.shape[0]
     block_links = coupling_listing[0]
     factor = taper_factors[0] / (members - 1)

time: 125 us -> 114 us (0.912)
  starting transfers between devices: 14.9 us -> 37.5 us
  waiting for transfers between devices: 46.4 us -> 28.1 us
  between operations: 14.3 us -> 1.03 us
  local copies, waits for them, and re-layouts: 6.04 us -> 14.1 us
  blocking collectives: 28.1 us -> 20.6 us
  matrix products: 7.11 us -> 4.88 us
    all_gather x1 -> x0, waiting for transfers between devices: 34.1 us -> none  [local(): all_products = lax.all_gather(products, 'obs', axis=0, tiled=True)]
    ppermute x0 -> x7, starting transfers between devices: none -> 22.6 us  [the longest x3 13.7 us: gather_around(): upper.append(lax.ppermute(upper[-1] if upper else x, axis, back))]
    ppermute x0 -> x7, waiting for transfers between devices: none -> 15.8 us  [the longest x4 15.8 us: gather_around(): lower.append(lax.ppermute(lower[-1] if lower else x, axis, pairs))]
    all_to_all x1, blocking collectives: 28.1 us -> 20.6 us  [local(): lax.all_to_all(increment_low, 'slab', split_axis=0, concat_axis=1, tiled=...]
    unnamed x21 -> x28, local copies, waits for them, and re-layouts: 2.31 us -> 7.38 us
    gather x0 -> x1, local copies, waits for them, and re-layouts: none -> 2.27 us  [gather_around(): tiles = tiles[(jnp.arange(devices) - shift) % devices]]
    dot_general x1, matrix products: 3.85 us -> 2.33 us  [local(): jnp.einsum('bc,cmn->bmn', localize, all_products, precision=highest)]
  transfers between devices with their start and end apart: 2 -> 8, of which waited for: 2 -> 5; matrix products, arithmetic and copies ran while one was open for 1% -> 5% of each run, Pallas kernels for 0% -> 0%
where the time goes in v1:
time: 114 us
  starting transfers between devices  37.5 us (33%)
  waiting for transfers between devices  28.1 us (25%)
  blocking collectives  20.6 us (18%)
  local copies, waits for them, and re-layouts  14.1 us (12%)
  other arithmetic  7.54 us (7%)
  matrix products  4.88 us (4%)
    all_to_all x1, blocking collectives, local(): lax.all_to_all(increment_low, 'slab', split_axis=0, concat_axis=1, tiled=...  20.6 us
    ppermute x4, waiting for transfers between devices, gather_around(): lower.append(lax.ppermute(lower[-1] if lower else x, axis, pairs))  15.8 us
    all_to_all x1, starting transfers between devices, local(): lax.all_to_all(work_low, 'slab', split_axis=1, concat_axis=0, tiled=True)  14.8 us
    ppermute x3, starting transfers between devices, gather_around(): upper.append(lax.ppermute(upper[-1] if upper else x, axis, back))  13.7 us
    all_to_all x1, waiting for transfers between devices, local(): lax.all_to_all(work_low, 'slab', split_axis=1, concat_axis=0, tiled=True)  12.3 us
    ppermute x4, starting transfers between devices, gather_around(): lower.append(lax.ppermute(lower[-1] if lower else x, axis, pairs))  8.93 us
    unnamed x28, local copies, waits for them, and re-layouts  7.38 us
    gather x2, local copies, waits for them, and re-layouts, block_products(): prior_value = jnp.take(tile_work, positions, axis=1)  2.99 us
  transfers between devices with their start and end apart: 8, of which 5 were waited for; matrix products, arithmetic and copies ran while one was open for 5% of the time, Pallas kernels for 0%

profile of v1, /device:TPU:1, one launch (start us, length us, event | category | flops | bytes accessed | tf_op | source)
XLA Modules:
  0.0 113.7 jit_solution(716650092378375689)
XLA Ops:
  0.0 0.0 copy-start.1
  0.0 0.0 copy-start.2
  0.0 1.4 %convert_element_type.60 = bf16[1,131072]{1,0:T(2,128)(2,1)S(1)} convert(f32[1,131072]{1,0:T(1,128)} %param.8) | non-fusion elementwise | flops 131072 | bytes 786432 | tf_op jit(solution)/shard_map/convert_element_type | solution.py:70
  1.4 0.5 broadcast.160
  2.0 2.1 %reduce.1 = bf16[64,2048]{1,0:T(8,128)(2,1)S(1)} reduce(bf16[64,1,2048]{2,1,0:T(2,128)(2,1)S(1)} %bitcast.66, bf16[]{:T(256)} %broadcast.160), dimensions={1}, to_apply=%bitcast.59.reduce_sub_computation | reduce | bytes 524290
  4.1 0.9 reshape.228
  5.0 14.8 %all-to-all-start = ((bf16[64,2,1024]{2,1,0:T(2,128)(2,1)}), bf16[64,2,1024]{2,1,0:T(2,128)(2,1)S(1)}, u32[]{:S(2)}, u32[]{:S(2)}) async-start(bf16[64,2,1024]{2,1,0:T(2,128)(2,1)} %reshape.228), calls=%async_computation | async-start | bytes 524288 | tf_op jit(solution)/shard_map/all_to_all | solution.py:71
  20.5 0.0 copy-done.1
  20.5 0.0 copy-done.2
  20.6 12.3 %all-to-all-done = bf16[64,2,1024]{2,1,0:T(2,128)(2,1)S(1)} async-done(((bf16[64,2,1024]{2,1,0:T(2,128)(2,1)}), bf16[64,2,1024]{2,1,0:T(2,128)(2,1)S(1)}, u32[]{:S(2)}, u32[]{:S(2)}) %all-to-all-start) | async-done | bytes 262176 | tf_op jit(solution)/shard_map/all_to_all | solution.py:71
  32.9 0.2 reshape.229
  33.1 0.5 copy.30
  33.7 0.1 convert_bitcast_fusion
  33.7 0.0 copy-start.3
  33.8 0.0 copy-start.6
  33.8 2.8 %gather_fusion = f32[1024,64]{1,0:T(8,128)S(1)} fusion(f32[64,2048]{0,1:T(8,128)S(1)} %convert_bitcast_fusion, s32[1024]{0:T(1024)S(1)} %broadcast_clamp_fusion), kind=kCustom, calls=%fused_computation | custom fusion | bytes 528384 | tf_op jit(solution)/shard_map/jit(_take)/gather | solution.py:43
  36.6 0.0 copy-start.5
  36.6 0.0 copy-start.4
  36.6 0.4 fusion.5
  37.0 0.5 multiply_reduce_fusion
  37.5 0.2 copy.34
  37.7 0.0 copy-done.3
  37.7 0.0 copy-done.6
  37.7 0.2 fusion.10
  37.9 3.2 %collective-permute-start = (f32[8,64,64]{2,1,0:T(8,128)S(1)}, f32[8,64,64]{2,1,0:T(8,128)S(1)}, u32[]{:S(2)}, u32[]{:S(2)}) collective-permute-start(f32[8,64,64]{2,1,0:T(8,128)S(1)} %fusion.10), channel_id=1, source_target_pairs={{0,1},{1,2},{2,3},{3,4},{4,5},{5,6},{6,7},{7,0},{8,9},{9,10},{10,1... | collective-permute-start | bytes 393224 | tf_op jit(solution)/shard_map/ppermute | solution.py:23
  41.1 0.0 copy-done.5
  41.2 8.3 %collective-permute-done = f32[8,64,64]{2,1,0:T(8,128)S(1)} collective-permute-done((f32[8,64,64]{2,1,0:T(8,128)S(1)}, f32[8,64,64]{2,1,0:T(8,128)S(1)}, u32[]{:S(2)}, u32[]{:S(2)}) %collective-permute-start) | collective-permute-done | bytes 131104 | tf_op jit(solution)/shard_map/ppermute | solution.py:23
  49.4 1.9 %collective-permute-start.1 = (f32[8,64,64]{2,1,0:T(8,128)S(1)}, f32[8,64,64]{2,1,0:T(8,128)S(1)}, u32[]{:S(2)}, u32[]{:S(2)}) collective-permute-start(f32[8,64,64]{2,1,0:T(8,128)S(1)} %collective-permute-done), channel_id=1, source_target_pairs={{0,1},{1,2},{2,3},{3,4},{4,5},{5,6},{6,7},{7,0},{8,9},{9,10},{10,1... | collective-permute-start | bytes 393224 | tf_op jit(solution)/shard_map/ppermute | solution.py:23
  51.4 0.1 copy.32
  51.5 0.0 copy-done.4
  51.5 0.1 copy.31
  51.5 0.1 select_reduce_fusion
  51.7 4.6 %collective-permute-start.4 = (f32[8,64,64]{2,1,0:T(8,128)S(1)}, f32[8,64,64]{2,1,0:T(8,128)S(1)}, u32[]{:S(2)}, u32[]{:S(2)}) collective-permute-start(f32[8,64,64]{2,1,0:T(8,128)S(1)} %fusion.10), channel_id=1, source_target_pairs={{1,0},{2,1},{3,2},{4,3},{5,4},{6,5},{7,6},{0,7},{9,8},{10,9},{11,1... | collective-permute-start | bytes 393224 | tf_op jit(solution)/shard_map/ppermute | solution.py:25
  56.3 3.3 %collective-permute-done.1 = f32[8,64,64]{2,1,0:T(8,128)S(1)} collective-permute-done((f32[8,64,64]{2,1,0:T(8,128)S(1)}, f32[8,64,64]{2,1,0:T(8,128)S(1)}, u32[]{:S(2)}, u32[]{:S(2)}) %collective-permute-start.1) | collective-permute-done | bytes 131104 | tf_op jit(solution)/shard_map/ppermute | solution.py:23
  59.6 1.9 %collective-permute-start.2 = (f32[8,64,64]{2,1,0:T(8,128)S(1)}, f32[8,64,64]{2,1,0:T(8,128)S(1)}, u32[]{:S(2)}, u32[]{:S(2)}) collective-permute-start(f32[8,64,64]{2,1,0:T(8,128)S(1)} %collective-permute-done.1), channel_id=1, source_target_pairs={{0,1},{1,2},{2,3},{3,4},{4,5},{5,6},{6,7},{7,0},{8,9},{9,10},{10,1... | collective-permute-start | bytes 393224 | tf_op jit(solution)/shard_map/ppermute | solution.py:23
  61.5 0.2 convert_reduce_fusion
  61.7 0.0 collective-permute-done.4
  61.7 4.6 %collective-permute-start.5 = (f32[8,64,64]{2,1,0:T(8,128)S(1)}, f32[8,64,64]{2,1,0:T(8,128)S(1)}, u32[]{:S(2)}, u32[]{:S(2)}) collective-permute-start(f32[8,64,64]{2,1,0:T(8,128)S(1)} %collective-permute-done.4), channel_id=1, source_target_pairs={{1,0},{2,1},{3,2},{4,3},{5,4},{6,5},{7,6},{0,7},{9,8},{10,9},{11,1... | collective-permute-start | bytes 393224 | tf_op jit(solution)/shard_map/ppermute | solution.py:25
  66.3 2.5 %collective-permute-done.2 = f32[8,64,64]{2,1,0:T(8,128)S(1)} collective-permute-done((f32[8,64,64]{2,1,0:T(8,128)S(1)}, f32[8,64,64]{2,1,0:T(8,128)S(1)}, u32[]{:S(2)}, u32[]{:S(2)}) %collective-permute-start.2) | collective-permute-done | bytes 131104 | tf_op jit(solution)/shard_map/ppermute | solution.py:23
  68.8 1.9 %collective-permute-start.3 = (f32[8,64,64]{2,1,0:T(8,128)S(1)}, f32[8,64,64]{2,1,0:T(8,128)S(1)}, u32[]{:S(2)}, u32[]{:S(2)}) collective-permute-start(f32[8,64,64]{2,1,0:T(8,128)S(1)} %collective-permute-done.2), channel_id=1, source_target_pairs={{0,1},{1,2},{2,3},{3,4},{4,5},{5,6},{6,7},{7,0},{8,9},{9,10},{10,1... | collective-permute-start | bytes 393224 | tf_op jit(solution)/shard_map/ppermute | solution.py:23
  70.7 0.1 div.45
  70.8 0.0 collective-permute-done.5
  70.8 4.6 %collective-permute-start.6 = (f32[8,64,64]{2,1,0:T(8,128)S(1)}, f32[8,64,64]{2,1,0:T(8,128)S(1)}, u32[]{:S(2)}, u32[]{:S(2)}) collective-permute-start(f32[8,64,64]{2,1,0:T(8,128)S(1)} %collective-permute-done.5), channel_id=1, source_target_pairs={{1,0},{2,1},{3,2},{4,3},{5,4},{6,5},{7,6},{0,7},{9,8},{10,9},{11,1... | collective-permute-start | bytes 393224 | tf_op jit(solution)/shard_map/ppermute | solution.py:25
  75.4 1.7 %collective-permute-done.3 = f32[8,64,64]{2,1,0:T(8,128)S(1)} collective-permute-done((f32[8,64,64]{2,1,0:T(8,128)S(1)}, f32[8,64,64]{2,1,0:T(8,128)S(1)}, u32[]{:S(2)}, u32[]{:S(2)}) %collective-permute-start.3) | collective-permute-done | bytes 131104 | tf_op jit(solution)/shard_map/ppermute | solution.py:23
  77.1 0.7 bitcast_dynamic-update-slice_fusion.7
  77.8 0.7 bitcast_dynamic-update-slice_fusion.6
  78.6 0.7 bitcast_dynamic-update-slice_fusion.5
  79.3 0.7 bitcast_dynamic-update-slice_fusion.4
  80.0 0.7 bitcast_dynamic-update-slice_fusion.3
  80.7 0.7 bitcast_dynamic-update-slice_fusion.2
  81.5 0.7 bitcast_dynamic-update-slice_fusion.1
  82.2 0.0 collective-permute-done.6
  82.2 0.7 bitcast_dynamic-update-slice_fusion
  82.9 2.3 %gather_fusion.1 = f32[8,8,64,64]{3,2,1,0:T(8,128)S(1)} fusion(f32[8,8,64,64]{3,2,1,0:T(8,128)} %bitcast_dynamic-update-slice_fusion, s32[1024]{0:T(1024)S(1)} %pad_clamp_fusion), kind=kCustom, calls=%fused_computation.1 | custom fusion | bytes 2097184 | tf_op jit(solution)/shard_map/gather | solution.py:28
  85.2 2.3 %fusion = f32[32,64,64]{2,0,1:T(8,128)S(1)} fusion(f32[64,64,64]{2,1,0:T(8,128)S(1)} %bitcast.62, f32[32,64]{1,0:T(8,128)S(1)} %select_reduce_fusion), kind=kOutput, calls=%fused_computation.2 | convolution fusion | flops 100663296 | bytes 1581056 | tf_op jit(solution)/shard_map/bc,cmn->bmn/dot_general | solution.py:90
  87.5 2.3 %convolution_convert_fusion = bf16[32,64,64]{2,1,0:T(8,128)(2,1)S(1)} fusion(f32[32,64,64]{2,0,1:T(8,128)S(1)} %fusion, f32[32,64]{1,0:T(8,128)S(1)} %div.45, bf16[64,32,64]{0,2,1:T(8,128)(2,1)S(1)} %bitcast.63), kind=kOutput, calls=%fused_computation.4 | convolution fusion | flops 101056512 | bytes 1056768 | tf_op jit(solution)/shard_map/bmn,nbp->mbp/dot_general | solution.py:92
  89.9 0.0 copy-start
  89.9 1.1 reduce.2
  91.0 0.2 copy.53
  91.2 0.2 reshape.230
  91.4 20.6 %all_to_all.23 = bf16[64,2,1024]{2,1,0:T(2,128)(2,1)S(1)} all-to-all(bf16[64,2,1024]{2,1,0:T(2,128)(2,1)S(1)} %reshape.230), channel_id=1, replica_groups=mesh['slab'=64,'obs'=8] {'slab'}, dimensions={0} | all-to-all | bytes 524288 | tf_op jit(solution)/shard_map/all_to_all | solution.py:94
  112.0 0.2 reshape.231
  112.2 0.0 copy-done
  112.2 1.5 %convert_add_fusion = f32[1,131072]{1,0:T(1,128)} fusion(f32[1,131072]{1,0:T(1,128)S(1)} %copy-done, bf16[1,131072]{1,0:T(2,128)(2,1)S(1)} %bitcast.65), kind=kLoop, calls=%fused_computation.7 | loop fusion | flops 262144 | bytes 1310720 | tf_op jit(solution)/shard_map/add | solution.py:95
  (13 shorter events, 0.1 us)
Async XLA Ops:
  0.0 20.5 %copy-start.1 = (bf16[64,1,1024]{2,0,1:T(8,128)(2,1)S(1)}, bf16[64,1,1024]{2,0,1:T(8,128)(2,1)}, u32[]{:S(2)}) copy-start(bf16[64,1,1024]{2,0,1:T(8,128)(2,1)} %param.9) | copy-start | bytes 393220
  0.0 20.5 %copy-start.2 = (s32[1,1024]{1,0:T(1,128)S(1)}, s32[1,1024]{1,0:T(1,128)}, u32[]{:S(2)}) copy-start(s32[1,1024]{1,0:T(1,128)} %param.12) | copy-start | bytes 12292
  5.0 27.9 %all-to-all-start = ((bf16[64,2,1024]{2,1,0:T(2,128)(2,1)}), bf16[64,2,1024]{2,1,0:T(2,128)(2,1)S(1)}, u32[]{:S(2)}, u32[]{:S(2)}) async-start(bf16[64,2,1024]{2,1,0:T(2,128)(2,1)} %reshape.228), calls=%async_computation | async-start | bytes 524288 | tf_op jit(solution)/shard_map/all_to_all | solution.py:71
  33.7 4.0 %copy-start.3 = (f32[1,1024]{1,0:T(1,128)S(1)}, f32[1,1024]{1,0:T(1,128)}, u32[]{:S(2)}) copy-start(f32[1,1024]{1,0:T(1,128)} %param.11) | copy-start | bytes 12292
  33.8 4.0 %copy-start.6 = (f32[1,1024]{1,0:T(1,128)S(1)}, f32[1,1024]{1,0:T(1,128)}, u32[]{:S(2)}) copy-start(f32[1,1024]{1,0:T(1,128)} %param.10) | copy-start | bytes 12292
  36.6 4.6 %copy-start.5 = (f32[1,32,8]{1,2,0:T(8,128)S(1)}, f32[1,32,8]{1,2,0:T(8,128)}, u32[]{:S(2)}) copy-start(f32[1,32,8]{1,2,0:T(8,128)} %param.15) | copy-start | bytes 3076
  36.6 14.9 %copy-start.4 = (s32[1,32,8]{1,2,0:T(8,128)S(1)}, s32[1,32,8]{1,2,0:T(8,128)}, u32[]{:S(2)}) copy-start(s32[1,32,8]{1,2,0:T(8,128)} %param.14) | copy-start | bytes 3076
  37.9 11.5 %collective-permute-start = (f32[8,64,64]{2,1,0:T(8,128)S(1)}, f32[8,64,64]{2,1,0:T(8,128)S(1)}, u32[]{:S(2)}, u32[]{:S(2)}) collective-permute-start(f32[8,64,64]{2,1,0:T(8,128)S(1)} %fusion.10), channel_id=1, source_target_pairs={{0,1},{1,2},{2,3},{3,4},{4,5},{5,6},{6,7},{7,0},{8,9},{9,10},{10,1... | collective-permute-start | bytes 393224 | tf_op jit(solution)/shard_map/ppermute | solution.py:23
  49.4 10.1 %collective-permute-start.1 = (f32[8,64,64]{2,1,0:T(8,128)S(1)}, f32[8,64,64]{2,1,0:T(8,128)S(1)}, u32[]{:S(2)}, u32[]{:S(2)}) collective-permute-start(f32[8,64,64]{2,1,0:T(8,128)S(1)} %collective-permute-done), channel_id=1, source_target_pairs={{0,1},{1,2},{2,3},{3,4},{4,5},{5,6},{6,7},{7,0},{8,9},{9,10},{10,1... | collective-permute-start | bytes 393224 | tf_op jit(solution)/shard_map/ppermute | solution.py:23
  51.7 10.0 %collective-permute-start.4 = (f32[8,64,64]{2,1,0:T(8,128)S(1)}, f32[8,64,64]{2,1,0:T(8,128)S(1)}, u32[]{:S(2)}, u32[]{:S(2)}) collective-permute-start(f32[8,64,64]{2,1,0:T(8,128)S(1)} %fusion.10), channel_id=1, source_target_pairs={{1,0},{2,1},{3,2},{4,3},{5,4},{6,5},{7,6},{0,7},{9,8},{10,9},{11,1... | collective-permute-start | bytes 393224 | tf_op jit(solution)/shard_map/ppermute | solution.py:25
  59.6 9.3 %collective-permute-start.2 = (f32[8,64,64]{2,1,0:T(8,128)S(1)}, f32[8,64,64]{2,1,0:T(8,128)S(1)}, u32[]{:S(2)}, u32[]{:S(2)}) collective-permute-start(f32[8,64,64]{2,1,0:T(8,128)S(1)} %collective-permute-done.1), channel_id=1, source_target_pairs={{0,1},{1,2},{2,3},{3,4},{4,5},{5,6},{6,7},{7,0},{8,9},{9,10},{10,1... | collective-permute-start | bytes 393224 | tf_op jit(solution)/shard_map/ppermute | solution.py:23
  61.7 9.1 %collective-permute-start.5 = (f32[8,64,64]{2,1,0:T(8,128)S(1)}, f32[8,64,64]{2,1,0:T(8,128)S(1)}, u32[]{:S(2)}, u32[]{:S(2)}) collective-permute-start(f32[8,64,64]{2,1,0:T(8,128)S(1)} %collective-permute-done.4), channel_id=1, source_target_pairs={{1,0},{2,1},{3,2},{4,3},{5,4},{6,5},{7,6},{0,7},{9,8},{10,9},{11,1... | collective-permute-start | bytes 393224 | tf_op jit(solution)/shard_map/ppermute | solution.py:25
  68.8 8.3 %collective-permute-start.3 = (f32[8,64,64]{2,1,0:T(8,128)S(1)}, f32[8,64,64]{2,1,0:T(8,128)S(1)}, u32[]{:S(2)}, u32[]{:S(2)}) collective-permute-start(f32[8,64,64]{2,1,0:T(8,128)S(1)} %collective-permute-done.2), channel_id=1, source_target_pairs={{0,1},{1,2},{2,3},{3,4},{4,5},{5,6},{6,7},{7,0},{8,9},{9,10},{10,1... | collective-permute-start | bytes 393224 | tf_op jit(solution)/shard_map/ppermute | solution.py:23
  70.8 11.4 %collective-permute-start.6 = (f32[8,64,64]{2,1,0:T(8,128)S(1)}, f32[8,64,64]{2,1,0:T(8,128)S(1)}, u32[]{:S(2)}, u32[]{:S(2)}) collective-permute-start(f32[8,64,64]{2,1,0:T(8,128)S(1)} %collective-permute-done.5), channel_id=1, source_target_pairs={{1,0},{2,1},{3,2},{4,3},{5,4},{6,5},{7,6},{0,7},{9,8},{10,9},{11,1... | collective-permute-start | bytes 393224 | tf_op jit(solution)/shard_map/ppermute | solution.py:25
  89.9 22.3 %copy-start = (f32[1,131072]{1,0:T(1,128)S(1)}, f32[1,131072]{1,0:T(1,128)}, u32[]{:S(2)}) copy-start(f32[1,131072]{1,0:T(1,128)} %param.8) | copy-start | bytes 1572868
